TPU v7x, 32 devices: a whole 2x2x4 slice. The times are simulated.
32 devices in a mesh: seq: 2 (over x), mp: 4 (over z), dp: 4 (over y, core).
Axes of the slice: x: 2, y: 2, z: 4, core: 2. Of those that a mesh axis runs over, the one named last changes fastest.
Arguments:
- features: bfloat16 [4, 2048, 768], P('dp', 'seq'), may hold values from -6 to 6
- conv_weight: bfloat16 [5, 768, 768], P(None, 'mp'), may hold values from -0.09375 to 0.09375
- keep: int32 [4], P('dp'), may hold values 0 or 1
- tiles: int32 [4, 2, 2, 2], P('dp'), may hold values from 0 to 63, as said below
- counts: int32 [4, 2], P('dp'), may hold values from 0 to 2, as said below
- targets: float32 [4, 2, 2, 1024], P('dp', 'seq'), may hold values from -6 to 6
Outputs:
- conv_grad: float32 [5, 768, 768], P(None, 'mp', ('seq', 'dp'))
Inputs may be any that keep to these rules, and one draw needn't show every extreme that they name: `tiles`: entries are block numbers of 32 positions in a sequence. For every sequence and owner, listing the 2 row blocks and then the 2 column blocks, exactly 2 of these 4 entries lie in the positions of each index of seq. Each owner's live slots are its first counts slots; in every sequence some owner has all 2 slots live.
All inputs are finite; a program needn't handle non-finite values. No bound on the sum of `keep` on one device may be relied on, other than what follows from the above.
Results may differ from a plain program's by a relative error of at most 0.0015.
Values may be sent and summed in bfloat16 or wider, within the bound.
No kernel may reach another device: no remote copies, remote signals or barrier semaphores. Data moves between devices by JAX's collectives and lax.ppermute only.
A program may use at most 64 MiB of HBM per device.

v0:
```python
import math
import jax
import jax.numpy as jnp
from jax import lax
from jax.sharding import PartitionSpec as P

TB = 32
PER = 2


def extended(cells, sides, width):
    for axis, dim in sides:
        count = lax.axis_size(axis)
        ends = count - 1
        head = lax.slice_in_dim(cells, 0, width, axis=dim)
        tail = lax.slice_in_dim(cells, cells.shape[dim] - width, cells.shape[dim], axis=dim)
        cells = jnp.concatenate(
            [
                lax.ppermute(tail, axis, [(i, (i + 1) % count) for i in range(ends)]),
                cells,
                lax.ppermute(head, axis, [((i + 1) % count, i) for i in range(ends)]),
            ],
            axis=dim,
        )
    return cells


def take_rows(source_array, index_array):
    return jax.vmap(lambda table, picked: table[picked])(source_array, index_array)


def conv_apply(padded, weight, length):
    total = jnp.einsum(
        "mbi,oi->mbo", padded[:, 0:length], weight[0], preferred_element_type=jnp.float32
    )
    for offset in range(1, weight.shape[0]):
        total = total + jnp.einsum(
            "mbi,oi->mbo",
            padded[:, offset : offset + length],
            weight[offset],
            preferred_element_type=jnp.float32,
        )
    return total


def weight_term(padded, dconv, length, taps):
    return jnp.stack(
        [
            jnp.einsum(
                "mbi,mbo->oi",
                padded[:, offset : offset + length],
                dconv,
                preferred_element_type=jnp.float32,
            )
            for offset in range(taps)
        ]
    )


def dense_path(features, conv_weight, keep, tiles, counts, targets):
    members, length, width = features.shape
    taps = conv_weight.shape[0]
    narrow = conv_weight.shape[1]
    seq_count = lax.axis_size("seq")
    my_index = lax.axis_index("seq")
    my_part = lax.axis_index("mp")
    x_float = features.astype(jnp.float32)
    activations = jax.nn.gelu(x_float).astype(jnp.bfloat16)
    padded = extended(activations, (("seq", 1),), 2)
    scaling = 1.25 * keep.astype(jnp.float32)
    conv_out = conv_apply(padded, conv_weight, length)
    x_local = lax.dynamic_slice_in_dim(x_float, my_part * narrow, narrow, 2)
    mixed_out = (x_local + scaling[:, None, None] * conv_out).astype(jnp.bfloat16)
    capacity = tiles.shape[2]
    n_sides = 2 * capacity
    per_block = length // TB
    sides = jnp.concatenate([tiles[..., 0], tiles[..., 1]], axis=-1)
    side_source = sides // per_block
    side_local = sides % per_block
    own_sides = lax.dynamic_index_in_dim(sides, my_index, 1, keepdims=False)
    own_source = own_sides // per_block
    before = jnp.arange(n_sides)[None, :] < jnp.arange(n_sides)[:, None]
    same_source = own_source[:, :, None] == own_source[:, None, :]
    rank_within = jnp.sum(jnp.logical_and(same_source, before[None]), axis=-1)
    slot_index = own_source * PER + rank_within
    held_here = side_source == my_index
    held_order = jnp.cumsum(held_here.astype(jnp.int32), axis=-1) - 1
    picks = jnp.stack(
        [
            jnp.sum(
                jnp.where(jnp.logical_and(held_here, held_order == position), side_local, 0),
                axis=-1,
            )
            for position in range(PER)
        ],
        axis=-1,
    )
    blocks = mixed_out.reshape(members, per_block, TB, narrow)
    whole = lax.all_gather(blocks, "seq", axis=1, tiled=True)
    side_rows = take_rows(whole, own_sides)
    row_side = side_rows[:, :capacity]
    col_side = side_rows[:, capacity:]
    partial_tiles = jnp.einsum(
        "mcid,mcjd->mcij", row_side, col_side, preferred_element_type=jnp.float32
    )
    predicted = lax.psum(partial_tiles, "mp") / math.sqrt(width)
    target_tiles = targets[:, 0].reshape(members, capacity, TB, TB)
    own_count = lax.dynamic_index_in_dim(counts, my_index, 1, keepdims=False)
    live_mask = (jnp.arange(capacity)[None, :] < own_count[:, None]).astype(jnp.float32)
    n_live = jnp.sum(counts, axis=-1).astype(jnp.float32)
    dpredicted = (
        2.0
        / math.sqrt(width)
        * live_mask[:, :, None, None]
        * (predicted - target_tiles)
        / n_live[:, None, None, None]
    )
    row_float = row_side.astype(jnp.float32)
    col_float = col_side.astype(jnp.float32)
    drow = jnp.einsum("mcij,mcjd->mcid", dpredicted, col_float, precision=lax.Precision.HIGHEST)
    dcol = jnp.einsum("mcij,mcid->mcjd", dpredicted, row_float, precision=lax.Precision.HIGHEST)
    dside = jnp.concatenate([drow, dcol], axis=1).astype(jnp.bfloat16)
    inverse = jnp.argsort(slot_index, axis=-1)
    outgoing_grads = take_rows(dside, inverse).reshape(members, seq_count, PER, TB, narrow)
    returned = lax.all_to_all(outgoing_grads, "seq", split_axis=1, concat_axis=1, tiled=True)
    selector = (
        picks.reshape(members, seq_count * PER)[:, :, None] == jnp.arange(per_block)[None, None, :]
    ).astype(jnp.bfloat16)
    dmixed = jnp.einsum(
        "mkn,mktd->mntd",
        selector,
        returned.reshape(members, seq_count * PER, TB, narrow),
        preferred_element_type=jnp.float32,
    ).reshape(members, length, narrow)
    dconv = (scaling[:, None, None] * dmixed).astype(jnp.bfloat16)
    weight_local = weight_term(padded, dconv, length, taps)
    return lax.psum_scatter(weight_local, ("seq", "dp"), scatter_dimension=2, tiled=True)


def axis_sum(value, axis):
    count = lax.axis_size(axis)
    total = value
    for shift in range(1, count):
        total = total + lax.ppermute(value, axis, [(i, (i + shift) % count) for i in range(count)])
    return total


def sparse_path(features, conv_weight, keep, tiles, counts, targets):
    _, length, width = features.shape
    taps, narrow, _ = conv_weight.shape
    halo = taps // 2
    span = TB + 2 * halo
    owners, capacity = (tiles.shape[1], tiles.shape[2])
    n_sides = 2 * capacity
    per_block = length // TB
    seq_count = lax.axis_size("seq")
    groups = lax.axis_size("dp")
    peers = seq_count * groups
    held = owners * PER
    cols = width // peers
    my_index = lax.axis_index("seq")
    my_part = lax.axis_index("mp")
    small = jnp.concatenate([tiles.reshape(-1), counts.reshape(-1), keep.reshape(-1)]).astype(
        jnp.float32
    )
    bundle = jnp.concatenate([targets.reshape(-1), small])
    gathered = lax.all_gather(bundle, ("seq", "dp")).reshape(seq_count, groups, -1)
    n_targets = capacity * TB * TB
    n_tiles = owners * capacity * 2
    meta = gathered[0, :, n_targets:].astype(jnp.int32)
    tiles_all = meta[:, :n_tiles].reshape(groups, owners, capacity, 2)
    counts_all = meta[:, n_tiles : n_tiles + owners]
    keep_all = meta[:, n_tiles + owners]
    targets_all = gathered[:, :, :n_targets]
    sides = jnp.concatenate([tiles_all[..., 0], tiles_all[..., 1]], axis=-1)
    source = sides // per_block
    local = sides % per_block
    before = jnp.arange(n_sides)[None, :] < jnp.arange(n_sides)[:, None]
    same_source = source[..., :, None] == source[..., None, :]
    rank = jnp.sum(jnp.logical_and(same_source, before), axis=-1)
    slot = (
        (source * groups + jnp.arange(groups)[:, None, None]) * held
        + jnp.arange(owners)[None, :, None] * PER
        + rank
    )
    mine = lax.dynamic_index_in_dim(
        jnp.stack([source, local, rank], 0), lax.axis_index("dp"), 1, keepdims=False
    )
    held_here = mine[0] == my_index
    picks = jnp.stack(
        [
            jnp.sum(jnp.where(jnp.logical_and(held_here, mine[2] == r), mine[1], 0), axis=-1)
            for r in range(PER)
        ],
        axis=-1,
    ).reshape(held)
    cells = features[0]
    ends = seq_count - 1
    head = lax.ppermute(cells[length - halo :], "seq", [(i, i + 1) for i in range(ends)])
    tail = lax.ppermute(cells[:halo], "seq", [(i + 1, i) for i in range(ends)])
    rows = picks[:, None] * TB - halo + jnp.arange(span)[None, :]
    inside = jnp.take(cells, jnp.clip(rows, 0, length - 1), axis=0)
    edge_rows = jnp.concatenate([head, tail], axis=0)
    edge_index = jnp.where(rows < 0, rows + halo, rows - length + halo)
    outside = jnp.take(edge_rows, jnp.clip(edge_index, 0, 2 * halo - 1), axis=0)
    in_range = jnp.logical_and(rows >= 0, rows < length)
    windows = jnp.where(in_range[..., None], inside, outside)
    x_float = windows.astype(jnp.float32)
    act = jax.nn.gelu(x_float).astype(jnp.bfloat16)
    conv_out = jnp.einsum(
        "hti,oi->hto", act[:, 0:TB], conv_weight[0], preferred_element_type=jnp.float32
    )
    for offset in range(1, taps):
        conv_out = conv_out + jnp.einsum(
            "hti,oi->hto",
            act[:, offset : offset + TB],
            conv_weight[offset],
            preferred_element_type=jnp.float32,
        )
    scaling = 1.25 * keep_all.astype(jnp.float32)
    my_scale = lax.dynamic_index_in_dim(scaling, lax.axis_index("dp"), 0, keepdims=False)
    x_part = lax.dynamic_slice_in_dim(x_float[:, halo : halo + TB], my_part * narrow, narrow, 2)
    mixed = (x_part + my_scale * conv_out).astype(jnp.bfloat16)
    act_cut = act.reshape(held, span, peers, cols).transpose(2, 0, 1, 3).reshape(peers, -1)
    mixed_rep = jnp.broadcast_to(mixed.reshape(1, -1), (peers, held * TB * narrow))
    outgoing = jnp.concatenate([mixed_rep, act_cut], axis=1)
    incoming = lax.all_to_all(outgoing, ("seq", "dp"), 0, 0, tiled=True)
    mixed_in = incoming[:, : held * TB * narrow].reshape(peers * held, TB, narrow)
    act_in = incoming[:, held * TB * narrow :].reshape(peers * held, span, cols)
    side_rows = jnp.take(mixed_in, slot, axis=0)
    row_side = side_rows[:, :, :capacity]
    col_side = side_rows[:, :, capacity:]
    partial_tiles = jnp.einsum(
        "qocid,qocjd->qocij", row_side, col_side, preferred_element_type=jnp.float32
    )
    predicted = axis_sum(partial_tiles, "mp") / math.sqrt(width)
    target_tiles = targets_all.reshape(seq_count, groups, capacity, TB, TB).transpose(1, 0, 2, 3, 4)
    live_mask = (jnp.arange(capacity)[None, None, :] < counts_all[:, :, None]).astype(jnp.float32)
    n_live = jnp.sum(counts_all, axis=-1).astype(jnp.float32)
    dpredicted = (
        2.0
        / math.sqrt(width)
        * live_mask[..., None, None]
        * (predicted - target_tiles)
        / n_live[:, None, None, None, None]
    )
    row_float = row_side.astype(jnp.float32)
    col_float = col_side.astype(jnp.float32)
    drow = jnp.einsum("qocij,qocjd->qocid", dpredicted, col_float, precision=lax.Precision.HIGHEST)
    dcol = jnp.einsum("qocij,qocid->qocjd", dpredicted, row_float, precision=lax.Precision.HIGHEST)
    grads = jnp.concatenate([drow, dcol], axis=2).astype(jnp.bfloat16).astype(jnp.float32)
    grads = grads.reshape(groups, owners * n_sides, TB, narrow)
    flat_sides = sides.reshape(groups, owners * n_sides)
    same_block = flat_sides[:, :, None] == flat_sides[:, None, :]
    total = jnp.sum(jnp.where(same_block[..., None, None], grads[:, None], 0.0), axis=2)
    earlier = jnp.arange(owners * n_sides)[None, :] < jnp.arange(owners * n_sides)[:, None]
    first = jnp.logical_not(jnp.any(jnp.logical_and(same_block, earlier[None]), axis=-1))
    dconv = (scaling[:, None, None, None] * total).astype(jnp.bfloat16)
    dconv = jnp.where(first[..., None, None], dconv, jnp.zeros_like(dconv))
    act_sides = jnp.take(act_in, slot.reshape(groups, owners * n_sides), axis=0)
    return jnp.stack(
        [
            jnp.einsum(
                "qato,qati->oi",
                dconv,
                act_sides[:, :, offset : offset + TB],
                preferred_element_type=jnp.float32,
            )
            for offset in range(taps)
        ]
    )


def per_device(features, conv_weight, keep, tiles, counts, targets):
    members, length, _ = features.shape
    owners, capacity = (tiles.shape[1], tiles.shape[2])
    fits = members == 1 and targets.shape[1] == 1 and (2 * owners * capacity * TB <= length)
    if fits:
        return sparse_path(features, conv_weight, keep, tiles, counts, targets)
    return dense_path(features, conv_weight, keep, tiles, counts, targets)


def solution(mesh):
    placed = (
        P("dp", "seq", None),
        P(None, "mp", None),
        P("dp"),
        P("dp", None, None, None),
        P("dp", None),
        P("dp", "seq", None, None),
    )
    return jax.shard_map(
        per_device,
        mesh=mesh,
        in_specs=placed,
        out_specs=P(None, "mp", ("seq", "dp")),
        check_vma=False,
    )
```

profile of v0, /device:TPU:0, one launch (start us, length us, event | category | flops | bytes accessed | tf_op | source)
XLA Modules:
  0.0 141.5 jit_solution(4417940106494104526)
XLA Ops:
  6.5 0.7 slice_bitcast_fusion.1
  7.3 4.8 %collective-permute-start = (bf16[2,768]{1,0:T(2,128)(2,1)S(1)}, bf16[2,768]{1,0:T(2,128)(2,1)S(1)}, u32[]{:S(2)}, u32[]{:S(2)}) collective-permute-start(bf16[2,768]{1,0:T(2,128)(2,1)S(1)} %get-tuple-element.11), channel_id=1, source_target_pairs={{0,16},{1,17},{2,18},{3,19},{4,20},{5,21},{6,22},{7,23},{8,24},{9,... | collective-permute-start | bytes 9224 | tf_op jit(solution)/shard_map/ppermute | solution.py:199
  12.1 1.3 collective-permute-start.1
  14.1 0.8 reshape.924
  14.8 0.7 copy.140
  15.5 1.2 dynamic-slice.1
  17.4 0.7 add_convert_fusion
  18.2 0.1 maximum_dynamic-update-slice_fusion
  18.3 0.6 copy-done
  19.2 51.9 %all-reduce.3.cloned.1.call-done = f32[16472]{0:T(1024)} async-done(((f32[16472]{0:T(1024)}), f32[16472]{0:T(1024)}) %all-reduce.3.cloned.1.call-update) | async-done | bytes 65904
  71.1 1.0 reshape.926
  72.2 0.2 fusion.81
  72.3 0.2 fusion.79
  72.6 0.1 copy.90
  73.1 0.3 convert_reduce_fusion
  73.7 0.2 select_reduce_fusion.2
  74.4 2.6 %gather_fusion = bf16[144,768]{1,0:T(8,128)(2,1)S(1)} fusion(bf16[1024,768]{1,0:T(8,128)(2,1)} %bitcast.114, s32[1024]{0:T(1024)S(1)} %pad_clamp_fusion.3), kind=kCustom, calls=%fused_computation | custom fusion | bytes 442944 | tf_op jit(solution)/shard_map/jit(_take)/gather | solution.py:202
  77.1 0.3 gather.22
  77.5 0.9 gather_fusion.1
  78.5 0.3 gather.23
  78.9 0.5 constant_dynamic-slice_fusion
  79.5 0.1 copy.100
  79.6 0.2 and_reduce_fusion
  80.1 0.1 copy.97
  80.2 0.2 reshape.930
  80.4 0.4 fusion.23
  80.8 0.4 reshape.928
  81.2 0.4 fusion.22
  81.6 0.9 copy-done.2
  82.6 0.2 fusion.29
  82.8 0.2 convolution_add_fusion.3
  83.1 0.2 convolution_add_fusion.2
  83.4 0.2 convolution_add_fusion.1
  83.6 0.9 fusion.2
  84.5 0.1 reshape.989
  84.8 0.5 broadcast.811
  85.3 1.1 reduce.4
  86.4 1.0 reshape.990
  87.4 3.9 %all-to-all-start = ((bf16[8,2,19200]{2,1,0:T(2,128)(2,1)}), bf16[8,2,19200]{2,1,0:T(2,128)(2,1)S(1)}, u32[]{:S(2)}, u32[]{:S(2)}) async-start(bf16[8,2,19200]{2,1,0:T(2,128)(2,1)} %reshape.990), calls=%async_computation | async-start | bytes 1228800 | tf_op jit(solution)/shard_map/all_to_all | solution.py:227
  91.4 9.7 %all-to-all-done = bf16[8,2,19200]{2,1,0:T(2,128)(2,1)S(1)} async-done(((bf16[8,2,19200]{2,1,0:T(2,128)(2,1)}), bf16[8,2,19200]{2,1,0:T(2,128)(2,1)S(1)}, u32[]{:S(2)}, u32[]{:S(2)}) %all-to-all-start) | async-done | bytes 614432 | tf_op jit(solution)/shard_map/all_to_all | solution.py:227
  101.1 0.5 reshape.991
  101.7 0.6 reshape.929
  102.4 0.6 gather_fusion.2
  102.9 0.1 broadcast_select_fusion
  103.1 0.2 fusion.50
  103.3 3.4 %collective-permute-start.4 = (f32[4,2,2,32,32]{4,3,2,1,0:T(8,128)S(1)}, f32[4,2,2,32,32]{4,3,2,1,0:T(8,128)S(1)}, u32[]{:S(2)}, u32[]{:S(2)}) collective-permute-start(f32[4,2,2,32,32]{4,3,2,1,0:T(8,128)S(1)} %fusion.50), channel_id=1, source_target_pairs={{0,12},{4,0},{8,4},{12,8},{1,13},{5,1},{9,5},{13,9},{2,14},{6,2},{... | collective-permute-start | bytes 196616 | tf_op jit(solution)/shard_map/ppermute | solution.py:144
  106.7 1.1 collective-permute-start.2
  107.8 0.4 reshape.931
  108.2 0.6 gather_fusion.3
  108.8 0.1 copy_select_fusion
  108.9 4.5 %collective-permute-done.4 = f32[4,2,2,32,32]{4,3,2,1,0:T(8,128)S(1)} collective-permute-done((f32[4,2,2,32,32]{4,3,2,1,0:T(8,128)S(1)}, f32[4,2,2,32,32]{4,3,2,1,0:T(8,128)S(1)}, u32[]{:S(2)}, u32[]{:S(2)}) %collective-permute-start.4) | collective-permute-done | bytes 65568 | tf_op jit(solution)/shard_map/ppermute | solution.py:144
  113.5 15.5 %collective-permute-done.3 = f32[4,2,2,32,32]{4,3,2,1,0:T(8,128)S(1)} collective-permute-done((f32[4,2,2,32,32]{4,3,2,1,0:T(8,128)S(1)}, f32[4,2,2,32,32]{4,3,2,1,0:T(8,128)S(1)}, u32[]{:S(2)}, u32[]{:S(2)}) %collective-permute-start.3) | collective-permute-done | bytes 65568 | tf_op jit(solution)/shard_map/ppermute | solution.py:144
  129.0 0.1 fusion.48
  129.1 0.4 convolution_convert_fusion
  129.5 0.3 convolution_convert_fusion.1
  130.0 0.1 convert.9
  130.1 1.4 select_reduce_fusion
  131.5 0.2 fusion.14
  131.7 0.3 fusion.7
  132.0 0.3 fusion.6
  132.3 0.3 fusion.5
  132.6 0.3 fusion.4
  133.0 0.8 copy-done.3
  133.7 1.0 fusion.3
  (62 shorter events, 2.6 us)
Async XLA Ops:
  6.5 64.6 %all-reduce.3.cloned.1.call-start = ((), (), s32[]{:S(2)}) async-start(), calls=%async_computation.1 | async-start | bytes 139264
  7.3 11.9 %collective-permute-start = (bf16[2,768]{1,0:T(2,128)(2,1)S(1)}, bf16[2,768]{1,0:T(2,128)(2,1)S(1)}, u32[]{:S(2)}, u32[]{:S(2)}) collective-permute-start(bf16[2,768]{1,0:T(2,128)(2,1)S(1)} %get-tuple-element.11), channel_id=1, source_target_pairs={{0,16},{1,17},{2,18},{3,19},{4,20},{5,21},{6,22},{7,23},{8,24},{9,... | collective-permute-start | bytes 9224 | tf_op jit(solution)/shard_map/ppermute | solution.py:199
  12.1 7.1 %collective-permute-start.1 = (bf16[2,768]{1,0:T(2,128)(2,1)S(1)}, bf16[2,768]{1,0:T(2,128)(2,1)S(1)}, u32[]{:S(2)}, u32[]{:S(2)}) collective-permute-start(bf16[2,768]{1,0:T(2,128)(2,1)S(1)} %get-tuple-element.12), channel_id=1, source_target_pairs={{16,0},{17,1},{18,2},{19,3},{20,4},{21,5},{22,6},{23,7},{24,8},{25... | collective-permute-start | bytes 9224 | tf_op jit(solution)/shard_map/ppermute | solution.py:200
  18.3 0.6 copy-start
  72.1 4.9 %copy-start.1 = (f32[2,4,2059]{2,1,0:T(4,128)}, f32[2,4,2059]{2,1,0:T(4,128)S(1)}, u32[]{:S(2)}) copy-start(f32[2,4,2059]{2,1,0:T(4,128)S(1)} %reshape.926) | copy-start | bytes 197668
  77.5 1.3 slice-start
  81.2 1.4 copy-start.2
  87.4 13.7 %all-to-all-start = ((bf16[8,2,19200]{2,1,0:T(2,128)(2,1)}), bf16[8,2,19200]{2,1,0:T(2,128)(2,1)S(1)}, u32[]{:S(2)}, u32[]{:S(2)}) async-start(bf16[8,2,19200]{2,1,0:T(2,128)(2,1)} %reshape.990), calls=%async_computation | async-start | bytes 1228800 | tf_op jit(solution)/shard_map/all_to_all | solution.py:227
  103.3 10.2 %collective-permute-start.4 = (f32[4,2,2,32,32]{4,3,2,1,0:T(8,128)S(1)}, f32[4,2,2,32,32]{4,3,2,1,0:T(8,128)S(1)}, u32[]{:S(2)}, u32[]{:S(2)}) collective-permute-start(f32[4,2,2,32,32]{4,3,2,1,0:T(8,128)S(1)} %fusion.50), channel_id=1, source_target_pairs={{0,12},{4,0},{8,4},{12,8},{1,13},{5,1},{9,5},{13,9},{2,14},{6,2},{... | collective-permute-start | bytes 196616 | tf_op jit(solution)/shard_map/ppermute | solution.py:144
  106.7 22.3 %collective-permute-start.3 = (f32[4,2,2,32,32]{4,3,2,1,0:T(8,128)S(1)}, f32[4,2,2,32,32]{4,3,2,1,0:T(8,128)S(1)}, u32[]{:S(2)}, u32[]{:S(2)}) collective-permute-start(f32[4,2,2,32,32]{4,3,2,1,0:T(8,128)S(1)} %fusion.50), channel_id=1, source_target_pairs={{0,8},{4,12},{8,0},{12,4},{1,9},{5,13},{9,1},{13,5},{2,10},{6,14},... | collective-permute-start | bytes 196616 | tf_op jit(solution)/shard_map/ppermute | solution.py:144
  106.7 22.3 %collective-permute-start.2 = (f32[4,2,2,32,32]{4,3,2,1,0:T(8,128)S(1)}, f32[4,2,2,32,32]{4,3,2,1,0:T(8,128)S(1)}, u32[]{:S(2)}, u32[]{:S(2)}) collective-permute-start(f32[4,2,2,32,32]{4,3,2,1,0:T(8,128)S(1)} %fusion.50), channel_id=1, source_target_pairs={{0,4},{4,8},{8,12},{12,0},{1,5},{5,9},{9,13},{13,1},{2,6},{6,10},{... | collective-permute-start | bytes 196616 | tf_op jit(solution)/shard_map/ppermute | solution.py:144
  132.9 0.8 copy-start.3
Sparse Core Ops, SparseCore 0:
  19.1 51.9 all-reduce.2
where the time goes:
time: 142 us
  waiting for transfers between devices  81.6 us (57%)
  local copies, waits for them, and re-layouts  18.4 us (13%)
  between operations  15.2 us (11%)
  starting transfers between devices  14.5 us (10%)
  other arithmetic  6.7 us (5%)
  matrix products  5.11 us (4%)
    unnamed x2, waiting for transfers between devices  51.9 us
    ppermute x3, waiting for transfers between devices, axis_sum(): lax.ppermute(value, axis, [(i, (i + shift) % count) for i in range(count)])  20 us
    all_to_all x1, waiting for transfers between devices, sparse_path(): incoming = lax.all_to_all(outgoing, ('seq', 'dp'), 0, 0, tiled=True)  9.65 us
    unnamed x14, local copies, waits for them, and re-layouts  5.84 us
    ppermute x1, starting transfers between devices, sparse_path(): lax.ppermute(cells[length - halo:], 'seq', [(i, i + 1) for i in range(end...  4.83 us
    ppermute x3, starting transfers between devices, axis_sum(): lax.ppermute(value, axis, [(i, (i + shift) % count) for i in range(count)])  4.48 us
    all_to_all x1, starting transfers between devices, sparse_path(): incoming = lax.all_to_all(outgoing, ('seq', 'dp'), 0, 0, tiled=True)  3.92 us
    gather x3, local copies, waits for them, and re-layouts, sparse_path(): inside = jnp.take(cells, jnp.clip(rows, 0, length - 1), axis=0)  3.02 us
  transfers between devices with their start and end apart: 7, of which 4 were waited for; matrix products, arithmetic and copies ran while one was open for 4% of the time, Pallas kernels for 0%

commit v1 on v0

--- a/solution.py
+++ b/solution.py
@@ -6,6 +6,18 @@
 
 TB = 32
 PER = 2
+
+
+def cut_along(array, dim, peers):
+    shape = array.shape
+    blocks = array.reshape(*shape[:dim], peers, shape[dim] // peers, *shape[dim + 1 :])
+    return jnp.moveaxis(blocks, dim, 0)
+
+
+def in_order(tiles, dim):
+    dims = list(tiles.shape[1:])
+    dims[dim] *= tiles.shape[0]
+    return jnp.moveaxis(tiles, 0, dim).reshape(dims)
 
 
 def extended(cells, sides, width):
@@ -224,7 +236,14 @@
     act_cut = act.reshape(held, span, peers, cols).transpose(2, 0, 1, 3).reshape(peers, -1)
     mixed_rep = jnp.broadcast_to(mixed.reshape(1, -1), (peers, held * TB * narrow))
     outgoing = jnp.concatenate([mixed_rep, act_cut], axis=1)
-    incoming = lax.all_to_all(outgoing, ("seq", "dp"), 0, 0, tiled=True)
+    size, here = (lax.axis_size(("seq", "dp")), lax.axis_index(("seq", "dp")))
+    pieces = cut_along(outgoing, 0, size)
+    outs = [pieces[here]]
+    for step in range(1, size):
+        sent = pieces[here ^ step]
+        outs.append(lax.ppermute(sent, ("seq", "dp"), [(i_2, i_2 ^ step) for i_2 in range(size)]))
+    pieces = jnp.stack(outs)[here ^ jnp.arange(size)]
+    incoming = in_order(pieces, 0)
     mixed_in = incoming[:, : held * TB * narrow].reshape(peers * held, TB, narrow)
     act_in = incoming[:, held * TB * narrow :].reshape(peers * held, span, cols)
     side_rows = jnp.take(mixed_in, slot, axis=0)

time: 142 us -> 146 us (1.028)
  starting transfers between devices: 14.5 us -> 18.3 us
  local copies, waits for them, and re-layouts: 18.4 us -> 20.4 us
    all_to_all x1 -> x0, waiting for transfers between devices: 9.65 us -> none  [sparse_path(): incoming = lax.all_to_all(outgoing, ('seq', 'dp'), 0, 0, tiled=True)]
    ppermute x0 -> x7, waiting for transfers between devices: none -> 8.73 us  [sparse_path(): lax.ppermute(sent, ('seq', 'dp'), [(i_2, i_2 ^ step) for i_2 in range(siz...]
    ppermute x0 -> x7, starting transfers between devices: none -> 7.68 us  [sparse_path(): lax.ppermute(sent, ('seq', 'dp'), [(i_2, i_2 ^ step) for i_2 in range(siz...]
    all_to_all x1 -> x0, starting transfers between devices: 3.92 us -> none  [sparse_path(): incoming = lax.all_to_all(outgoing, ('seq', 'dp'), 0, 0, tiled=True)]
    another operation x0 -> x1, local copies, waits for them, and re-layouts: none -> 1.89 us  [sparse_path(): pieces = jnp.stack(outs)[here ^ jnp.arange(size)]]
    unnamed x14 -> x11, local copies, waits for them, and re-layouts: 5.84 us -> 4.3 us
  transfers between devices with their start and end apart: 7 -> 13, of which waited for: 4 -> 6; matrix products, arithmetic and copies ran while one was open for 4% -> 4% of each run, Pallas kernels for 0% -> 0%
where the time goes in v1:
time: 146 us; the launch traced here: 145 us
  waiting for transfers between devices  80.6 us (55%)
  local copies, waits for them, and re-layouts  20.4 us (14%)
  starting transfers between devices  18.3 us (13%)
  between operations  15.3 us (10%)
  other arithmetic  5.59 us (4%)
  matrix products  5.1 us (3%)
    unnamed x2, waiting for transfers between devices  51.9 us
    ppermute x3, waiting for transfers between devices, axis_sum(): lax.ppermute(value, axis, [(i, (i + shift) % count) for i in range(count)])  19.9 us
    ppermute x7, waiting for transfers between devices, sparse_path(): lax.ppermute(sent, ('seq', 'dp'), [(i_2, i_2 ^ step) for i_2 in range(siz...  8.73 us
    ppermute x7, starting transfers between devices, sparse_path(): lax.ppermute(sent, ('seq', 'dp'), [(i_2, i_2 ^ step) for i_2 in range(siz...  7.68 us
    ppermute x1, starting transfers between devices, sparse_path(): lax.ppermute(cells[length - halo:], 'seq', [(i, i + 1) for i in range(end...  4.83 us
    ppermute x3, starting transfers between devices, axis_sum(): lax.ppermute(value, axis, [(i, (i + shift) % count) for i in range(count)])  4.5 us
    unnamed x11, local copies, waits for them, and re-layouts  4.3 us
    gather x3, local copies, waits for them, and re-layouts, sparse_path(): inside = jnp.take(cells, jnp.clip(rows, 0, length - 1), axis=0)  3.02 us
  transfers between devices with their start and end apart: 13, of which 6 were waited for; matrix products, arithmetic and copies ran while one was open for 4% of the time, Pallas kernels for 0%

profile of v1, /device:TPU:0, one launch (start us, length us, event | category | flops | bytes accessed | tf_op | source)
XLA Modules:
  0.0 145.2 jit_solution(13322846227891005172)
XLA Ops:
  6.5 0.7 slice_bitcast_fusion.1
  7.3 4.8 %collective-permute-start = (bf16[2,768]{1,0:T(2,128)(2,1)S(1)}, bf16[2,768]{1,0:T(2,128)(2,1)S(1)}, u32[]{:S(2)}, u32[]{:S(2)}) collective-permute-start(bf16[2,768]{1,0:T(2,128)(2,1)S(1)} %get-tuple-element.11), channel_id=1, source_target_pairs={{0,16},{1,17},{2,18},{3,19},{4,20},{5,21},{6,22},{7,23},{8,24},{9,... | collective-permute-start | bytes 9224 | tf_op jit(solution)/shard_map/ppermute | solution.py:211
  12.1 1.3 collective-permute-start.1
  14.1 0.8 reshape.957
  14.8 0.7 copy.93
  15.5 1.2 dynamic-slice.12
  17.4 0.7 add_convert_fusion
  18.2 0.1 maximum_dynamic-update-slice_fusion
  18.3 0.6 copy-done.1
  19.3 51.9 %all-reduce.3.cloned.1.call-done = f32[16472]{0:T(1024)} async-done(((f32[16472]{0:T(1024)}), f32[16472]{0:T(1024)}) %all-reduce.3.cloned.1.call-update) | async-done | bytes 65904
  71.1 1.0 reshape.959
  72.1 0.2 fusion.82
  72.3 0.2 fusion.80
  73.1 0.3 convert_reduce_fusion
  73.8 0.2 select_reduce_fusion.2
  74.4 2.6 %gather_fusion = bf16[144,768]{1,0:T(8,128)(2,1)S(1)} fusion(bf16[1024,768]{1,0:T(8,128)(2,1)} %bitcast.122, s32[1024]{0:T(1024)S(1)} %pad_clamp_fusion.4), kind=kCustom, calls=%fused_computation | custom fusion | bytes 442944 | tf_op jit(solution)/shard_map/jit(_take)/gather | solution.py:214
  77.1 0.3 gather.25
  77.6 0.9 gather_fusion.1
  78.5 0.3 gather.26
  78.9 0.5 constant_dynamic-slice_fusion.7
  79.6 0.4 fusion.23
  80.1 0.4 reshape.961
  80.4 0.4 fusion.22
  80.9 0.9 copy-done.2
  81.8 0.2 fusion.29
  82.1 0.2 convolution_add_fusion.3
  82.3 0.2 convolution_add_fusion.2
  82.6 0.2 convolution_add_fusion.1
  82.8 0.9 fusion.2
  83.7 0.1 reshape.1034
  84.0 1.3 constant_dynamic-slice_fusion
  85.3 2.7 %collective-permute-start.8 = (bf16[1,38400]{1,0:T(2,128)(2,1)S(1)}, bf16[1,38400]{1,0:T(2,128)(2,1)S(1)}, u32[]{:S(2)}, u32[]{:S(2)}) collective-permute-start(bf16[1,38400]{1,0:T(2,128)(2,1)S(1)} %get-tuple-element.13), channel_id=1, source_target_pairs={{0,19},{1,18},{2,17},{3,16},{16,3},{17,2},{18,1},{19,0},{4,23},{5,... | collective-permute-start | bytes 230408 | tf_op jit(solution)/shard_map/ppermute | solution.py:244
  88.0 1.4 collective-permute-start.7
  89.4 0.2 and_reduce_fusion
  90.1 0.2 reshape.964
  90.4 0.6 collective-permute-start.5
  91.0 1.4 collective-permute-start.4
  92.4 1.4 collective-permute-start.3
  93.8 3.2 %collective-permute-done.7 = bf16[1,38400]{1,0:T(2,128)(2,1)S(1)} collective-permute-done((bf16[1,38400]{1,0:T(2,128)(2,1)S(1)}, bf16[1,38400]{1,0:T(2,128)(2,1)S(1)}, u32[]{:S(2)}, u32[]{:S(2)}) %collective-permute-start.7) | collective-permute-done | bytes 76832 | tf_op jit(solution)/shard_map/ppermute | solution.py:244
  97.1 1.8 %collective-permute-done.6 = bf16[1,38400]{1,0:T(2,128)(2,1)S(1)} collective-permute-done((bf16[1,38400]{1,0:T(2,128)(2,1)S(1)}, bf16[1,38400]{1,0:T(2,128)(2,1)S(1)}, u32[]{:S(2)}, u32[]{:S(2)}) %collective-permute-start.6) | collective-permute-done | bytes 76832 | tf_op jit(solution)/shard_map/ppermute | solution.py:244
  98.9 3.7 %collective-permute-done.5 = bf16[1,38400]{1,0:T(2,128)(2,1)S(1)} collective-permute-done((bf16[1,38400]{1,0:T(2,128)(2,1)S(1)}, bf16[1,38400]{1,0:T(2,128)(2,1)S(1)}, u32[]{:S(2)}, u32[]{:S(2)}) %collective-permute-start.5) | collective-permute-done | bytes 76832 | tf_op jit(solution)/shard_map/ppermute | solution.py:244
  102.6 1.9 %stack.71 = bf16[8,1,38400]{2,0,1:T(8,128)(2,1)S(1)} concatenate(bf16[1,1,38400]{2,0,1:T(2,128)(2,1)S(1)} %get-tuple-element.20, bf16[1,1,38400]{2,0,1:T(2,128)(2,1)S(1)} %bitcast.132, bf16[1,1,38400]{2,0,1:T(2,128)(2,1)S(1)} %bitcast.131, bf16[1,1,38400]{2,0,1:T(2,128)(2,1)S(1)} %bitcast.130, bf16[1,1,38400]{2,0,1:T(2,128)(2,1)S(1)} %bitcast.129, ...), dimensions={0} | concatenate | bytes 1228800 | tf_op jit(solution)/shard_map/stack | solution.py:245
  104.5 1.0 gather_fusion.2
  105.5 0.6 reshape.963
  106.1 0.6 gather_fusion.3
  106.7 0.1 broadcast_select_fusion
  106.8 0.2 fusion.50
  107.1 3.4 %collective-permute-start.11 = (f32[4,2,2,32,32]{4,3,2,1,0:T(8,128)S(1)}, f32[4,2,2,32,32]{4,3,2,1,0:T(8,128)S(1)}, u32[]{:S(2)}, u32[]{:S(2)}) collective-permute-start(f32[4,2,2,32,32]{4,3,2,1,0:T(8,128)S(1)} %fusion.50), channel_id=1, source_target_pairs={{0,12},{4,0},{8,4},{12,8},{1,13},{5,1},{9,5},{13,9},{2,14},{6,2},{... | collective-permute-start | bytes 196616 | tf_op jit(solution)/shard_map/ppermute | solution.py:156
  110.5 1.1 collective-permute-start.9
  111.6 0.4 reshape.965
  112.0 0.6 gather_fusion.4
  112.7 4.5 %collective-permute-done.11 = f32[4,2,2,32,32]{4,3,2,1,0:T(8,128)S(1)} collective-permute-done((f32[4,2,2,32,32]{4,3,2,1,0:T(8,128)S(1)}, f32[4,2,2,32,32]{4,3,2,1,0:T(8,128)S(1)}, u32[]{:S(2)}, u32[]{:S(2)}) %collective-permute-start.11) | collective-permute-done | bytes 65568 | tf_op jit(solution)/shard_map/ppermute | solution.py:156
  117.2 15.4 %collective-permute-done.10 = f32[4,2,2,32,32]{4,3,2,1,0:T(8,128)S(1)} collective-permute-done((f32[4,2,2,32,32]{4,3,2,1,0:T(8,128)S(1)}, f32[4,2,2,32,32]{4,3,2,1,0:T(8,128)S(1)}, u32[]{:S(2)}, u32[]{:S(2)}) %collective-permute-start.10) | collective-permute-done | bytes 65568 | tf_op jit(solution)/shard_map/ppermute | solution.py:156
  132.7 0.1 fusion.48
  132.8 0.4 convolution_convert_fusion
  133.2 0.3 convolution_convert_fusion.1
  133.8 1.4 select_reduce_fusion
  135.2 0.2 fusion.14
  135.4 0.3 fusion.7
  135.7 0.3 fusion.6
  136.0 0.3 fusion.5
  136.3 0.3 fusion.4
  136.7 0.8 copy-done.3
  137.4 1.0 fusion.3
  (74 shorter events, 3.1 us)
Async XLA Ops:
  6.5 64.6 %all-reduce.3.cloned.1.call-start = ((), (), s32[]{:S(2)}) async-start(), calls=%async_computation | async-start | bytes 139264
  7.3 12.0 %collective-permute-start = (bf16[2,768]{1,0:T(2,128)(2,1)S(1)}, bf16[2,768]{1,0:T(2,128)(2,1)S(1)}, u32[]{:S(2)}, u32[]{:S(2)}) collective-permute-start(bf16[2,768]{1,0:T(2,128)(2,1)S(1)} %get-tuple-element.11), channel_id=1, source_target_pairs={{0,16},{1,17},{2,18},{3,19},{4,20},{5,21},{6,22},{7,23},{8,24},{9,... | collective-permute-start | bytes 9224 | tf_op jit(solution)/shard_map/ppermute | solution.py:211
  12.1 7.1 %collective-permute-start.1 = (bf16[2,768]{1,0:T(2,128)(2,1)S(1)}, bf16[2,768]{1,0:T(2,128)(2,1)S(1)}, u32[]{:S(2)}, u32[]{:S(2)}) collective-permute-start(bf16[2,768]{1,0:T(2,128)(2,1)S(1)} %get-tuple-element.12), channel_id=1, source_target_pairs={{16,0},{17,1},{18,2},{19,3},{20,4},{21,5},{22,6},{23,7},{24,8},{25... | collective-permute-start | bytes 9224 | tf_op jit(solution)/shard_map/ppermute | solution.py:212
  18.3 0.6 copy-start.1
  80.4 1.4 copy-start.2
  85.3 7.1 %collective-permute-start.8 = (bf16[1,38400]{1,0:T(2,128)(2,1)S(1)}, bf16[1,38400]{1,0:T(2,128)(2,1)S(1)}, u32[]{:S(2)}, u32[]{:S(2)}) collective-permute-start(bf16[1,38400]{1,0:T(2,128)(2,1)S(1)} %get-tuple-element.13), channel_id=1, source_target_pairs={{0,19},{1,18},{2,17},{3,16},{16,3},{17,2},{18,1},{19,0},{4,23},{5,... | collective-permute-start | bytes 230408 | tf_op jit(solution)/shard_map/ppermute | solution.py:244
  88.0 9.1 %collective-permute-start.7 = (bf16[1,38400]{1,0:T(2,128)(2,1)S(1)}, bf16[1,38400]{1,0:T(2,128)(2,1)S(1)}, u32[]{:S(2)}, u32[]{:S(2)}) collective-permute-start(bf16[1,38400]{1,0:T(2,128)(2,1)S(1)} %get-tuple-element.14), channel_id=1, source_target_pairs={{0,18},{1,19},{2,16},{3,17},{16,2},{17,3},{18,0},{19,1},{4,22},{5,... | collective-permute-start | bytes 230408 | tf_op jit(solution)/shard_map/ppermute | solution.py:244
  90.3 8.6 %collective-permute-start.6 = (bf16[1,38400]{1,0:T(2,128)(2,1)S(1)}, bf16[1,38400]{1,0:T(2,128)(2,1)S(1)}, u32[]{:S(2)}, u32[]{:S(2)}) collective-permute-start(bf16[1,38400]{1,0:T(2,128)(2,1)S(1)} %get-tuple-element.15), channel_id=1, source_target_pairs={{0,17},{1,16},{2,19},{3,18},{16,1},{17,0},{18,3},{19,2},{4,21},{5,... | collective-permute-start | bytes 230408 | tf_op jit(solution)/shard_map/ppermute | solution.py:244
  90.4 12.2 %collective-permute-start.5 = (bf16[1,38400]{1,0:T(2,128)(2,1)S(1)}, bf16[1,38400]{1,0:T(2,128)(2,1)S(1)}, u32[]{:S(2)}, u32[]{:S(2)}) collective-permute-start(bf16[1,38400]{1,0:T(2,128)(2,1)S(1)} %get-tuple-element.16), channel_id=1, source_target_pairs={{0,16},{1,17},{2,18},{3,19},{16,0},{17,1},{18,2},{19,3},{4,20},{5,... | collective-permute-start | bytes 230408 | tf_op jit(solution)/shard_map/ppermute | solution.py:244
  91.0 11.6 %collective-permute-start.4 = (bf16[1,38400]{1,0:T(2,128)(2,1)S(1)}, bf16[1,38400]{1,0:T(2,128)(2,1)S(1)}, u32[]{:S(2)}, u32[]{:S(2)}) collective-permute-start(bf16[1,38400]{1,0:T(2,128)(2,1)S(1)} %get-tuple-element.17), channel_id=1, source_target_pairs={{0,3},{1,2},{2,1},{3,0},{16,19},{17,18},{18,17},{19,16},{4,7},{5,6... | collective-permute-start | bytes 230408 | tf_op jit(solution)/shard_map/ppermute | solution.py:244
  92.4 10.2 %collective-permute-start.3 = (bf16[1,38400]{1,0:T(2,128)(2,1)S(1)}, bf16[1,38400]{1,0:T(2,128)(2,1)S(1)}, u32[]{:S(2)}, u32[]{:S(2)}) collective-permute-start(bf16[1,38400]{1,0:T(2,128)(2,1)S(1)} %get-tuple-element.18), channel_id=1, source_target_pairs={{0,2},{1,3},{2,0},{3,1},{16,18},{17,19},{18,16},{19,17},{4,6},{5,7... | collective-permute-start | bytes 230408 | tf_op jit(solution)/shard_map/ppermute | solution.py:244
  97.1 5.5 %collective-permute-start.2 = (bf16[1,38400]{1,0:T(2,128)(2,1)S(1)}, bf16[1,38400]{1,0:T(2,128)(2,1)S(1)}, u32[]{:S(2)}, u32[]{:S(2)}) collective-permute-start(bf16[1,38400]{1,0:T(2,128)(2,1)S(1)} %get-tuple-element.19), channel_id=1, source_target_pairs={{0,1},{1,0},{2,3},{3,2},{16,17},{17,16},{18,19},{19,18},{4,5},{5,4... | collective-permute-start | bytes 230408 | tf_op jit(solution)/shard_map/ppermute | solution.py:244
  105.5 1.2 copy-start
  106.7 4.9 %slice-start = ((bf16[8,38400]{1,0:T(8,128)(2,1)}), bf16[8,13824]{1,0:T(8,128)(2,1)S(1)}, s32[]{:S(2)}) async-start(bf16[8,38400]{1,0:T(8,128)(2,1)} %copy-done), calls=%async_computation.1 | async-start | bytes 442368 | tf_op jit(solution)/shard_map/slice | solution.py:248
  107.1 10.2 %collective-permute-start.11 = (f32[4,2,2,32,32]{4,3,2,1,0:T(8,128)S(1)}, f32[4,2,2,32,32]{4,3,2,1,0:T(8,128)S(1)}, u32[]{:S(2)}, u32[]{:S(2)}) collective-permute-start(f32[4,2,2,32,32]{4,3,2,1,0:T(8,128)S(1)} %fusion.50), channel_id=1, source_target_pairs={{0,12},{4,0},{8,4},{12,8},{1,13},{5,1},{9,5},{13,9},{2,14},{6,2},{... | collective-permute-start | bytes 196616 | tf_op jit(solution)/shard_map/ppermute | solution.py:156
  110.5 22.2 %collective-permute-start.10 = (f32[4,2,2,32,32]{4,3,2,1,0:T(8,128)S(1)}, f32[4,2,2,32,32]{4,3,2,1,0:T(8,128)S(1)}, u32[]{:S(2)}, u32[]{:S(2)}) collective-permute-start(f32[4,2,2,32,32]{4,3,2,1,0:T(8,128)S(1)} %fusion.50), channel_id=1, source_target_pairs={{0,8},{4,12},{8,0},{12,4},{1,9},{5,13},{9,1},{13,5},{2,10},{6,14},... | collective-permute-start | bytes 196616 | tf_op jit(solution)/shard_map/ppermute | solution.py:156
  110.5 22.2 %collective-permute-start.9 = (f32[4,2,2,32,32]{4,3,2,1,0:T(8,128)S(1)}, f32[4,2,2,32,32]{4,3,2,1,0:T(8,128)S(1)}, u32[]{:S(2)}, u32[]{:S(2)}) collective-permute-start(f32[4,2,2,32,32]{4,3,2,1,0:T(8,128)S(1)} %fusion.50), channel_id=1, source_target_pairs={{0,4},{4,8},{8,12},{12,0},{1,5},{5,9},{9,13},{13,1},{2,6},{6,10},{... | collective-permute-start | bytes 196616 | tf_op jit(solution)/shard_map/ppermute | solution.py:156
  136.7 0.8 copy-start.3
Sparse Core Ops, SparseCore 0:
  19.1 51.9 all-reduce.2
